TPU v7x, 32 devices: a whole 2x2x4 slice. The times are simulated.
32 devices in a mesh: req: 8 (over y, x, core), hid: 4 (over z).
Axes of the slice: x: 2, y: 2, z: 4, core: 2. Of those that a mesh axis runs over, the one named last changes fastest.
Arguments:
- hidden_in: bfloat16 [2048, 1024], P('req', 'hid'), may hold values from -6 to 6
- segments: int32 [8, 256], P('req'), may hold values from 0 to 7, never falling along the last dimension, each value on 1 to 128 neighbouring positions
- prefix_group: int32 [8, 8], P('req'), may hold values from 0 to 15
- prefix_cache: bfloat16 [16, 1024, 8, 128], P('req', None, 'hid'), may hold values from -400 to 400
- page_table: int32 [8, 2], P('req'), may hold values from 0 to 1, each once within a row
- norm_gain: float32 [1024], replicated, may hold values from 0.1 to 1.9
- w_query: bfloat16 [1024, 1024], P(None, 'hid'), may hold values from -0.1875 to 0.1875
- w_keyval: bfloat16 [1024, 1024], P(None, 'hid'), may hold values from -0.1875 to 0.1875
- w_out: bfloat16 [1024, 1024], P('hid'), may hold values from -0.1875 to 0.1875
- moe_gain: float32 [1024], replicated, may hold values from 0.1 to 1.9
- routes: int32 [2048, 8], P('req'), may hold values from 0 to 15, all different within a row; in each aligned block of 256 rows (0 to 255, 256 to 511, ...) at most 256 rows name the same one
- gates: float32 [2048, 8], P('req'), may hold values from 0.05 to 0.5
- w_gate_up: bfloat16 [16, 2, 1024, 512], P('req', None, None, 'hid'), may hold values from -0.1875 to 0.1875
- w_down: bfloat16 [16, 512, 1024], P('req', 'hid'), may hold values from -0.25 to 0.25
Outputs:
- hidden_out: bfloat16 [2048, 1024], P('req', 'hid')
- kv_pages: bfloat16 [16, 128, 8, 128], P('req', None, 'hid')
Inputs may be any that keep to these rules, and one draw needn't show every extreme that they name: `routes`: within the 256 rows of one row of the stream no expert is named by more than 256 tokens. `page_table`: each row is a permutation of 0 to 1. `segments`: segment numbers of a row never fall; each of the 8 documents has 1 to 128 tokens.
All inputs are finite; a program needn't handle non-finite values.
Results may differ from a plain program's by a relative error of at most 0.013.
Values may be sent and summed in bfloat16 or wider, within the bound.
No kernel may reach another device: no remote copies, remote signals or barrier semaphores. Data moves between devices by JAX's collectives and lax.ppermute only.
A program may use at most 128 MiB of HBM per device.

v0:
```python
import jax
import jax.numpy as jnp
from jax import lax
from jax.sharding import PartitionSpec as P

PAGE = 128


EPSILON = 1e-06
THETA = 10000.0


def rms_scale(row_data, gain_row):
    floats = row_data.astype(jnp.float32)
    mean_square = jnp.mean(floats * floats, axis=-1, keepdims=True)
    return (floats * lax.rsqrt(mean_square + EPSILON) * gain_row).astype(jnp.bfloat16)


def rotate(features, positions):
    half_dim = features.shape[-1] // 2
    frequency = THETA ** (-2.0 * jnp.arange(half_dim, dtype=jnp.float32) / features.shape[-1])
    angles = positions.astype(jnp.float32)[:, None] * frequency[None, :]
    cosine = jnp.cos(angles)[:, None, :]
    sine_part = jnp.sin(angles)[:, None, :]
    front_half = features[..., :half_dim]
    second = features[..., half_dim:]
    return jnp.concatenate(
        [front_half * cosine - second * sine_part, second * cosine + front_half * sine_part],
        axis=-1,
    )


def positions_of(segment_row, offset):
    earlier = jnp.sum((segment_row[None, :] < segment_row[:, None]).astype(jnp.int32), axis=1)
    token_index = jnp.arange(segment_row.shape[0], dtype=jnp.int32)
    return token_index - earlier + offset


def slots_of(route_rows, experts):
    flat_routes = route_rows.reshape(-1)
    onehot = (flat_routes[:, None] == jnp.arange(experts, dtype=jnp.int32)[None, :]).astype(
        jnp.int32
    )
    before = jnp.cumsum(onehot, axis=0) - onehot
    return (flat_routes, jnp.sum(before * onehot, axis=1))


def expert_rows(received, gate_up, down_proj):
    local_experts = down_proj.shape[0]
    slot_count = received.shape[1]
    model_width = received.shape[2]
    grouped = received.reshape(-1, local_experts, slot_count, model_width)
    gate_proj = jnp.einsum(
        "recd,edf->recf", grouped, gate_up[:, 0], preferred_element_type=jnp.float32
    )
    up_proj = jnp.einsum(
        "recd,edf->recf", grouped, gate_up[:, 1], preferred_element_type=jnp.float32
    )
    hidden = (jax.nn.silu(gate_proj) * up_proj).astype(jnp.bfloat16)
    produced = jnp.einsum("recf,efd->recd", hidden, down_proj, preferred_element_type=jnp.float32)
    return produced.reshape(-1, slot_count, model_width)


def shards(
    hidden_in,
    segments,
    prefix_group,
    prefix_cache,
    page_table,
    norm_gain,
    w_query,
    w_keyval,
    w_out,
    moe_gain,
    routes,
    gates,
    w_gate_up,
    w_down,
):
    req_count = lax.axis_size("req")
    whole = lax.all_gather(hidden_in, "hid", axis=1, tiled=True)
    tok_count = whole.shape[0]
    model_width = whole.shape[1]
    segment_row = segments[0]
    prefix_len = prefix_cache.shape[1]
    kv_heads = prefix_cache.shape[2]
    head_dim = prefix_cache.shape[3] // 2
    score_scale = head_dim ** (-0.5)
    normed = rms_scale(whole, norm_gain)
    position = positions_of(segment_row, prefix_len)
    projected = jnp.dot(normed, w_query, preferred_element_type=jnp.float32).reshape(
        tok_count, -1, head_dim
    )
    queries = rotate(projected, position).astype(jnp.bfloat16)
    q_groups = queries.shape[1] // kv_heads
    grouped_query = queries.reshape(tok_count, kv_heads, q_groups, head_dim)
    key_value = jnp.dot(normed, w_keyval, preferred_element_type=jnp.float32).reshape(
        tok_count, kv_heads, 2 * head_dim
    )
    key_rows = rotate(key_value[..., :head_dim], position).astype(jnp.bfloat16)
    value_rows = key_value[..., head_dim:].astype(jnp.bfloat16)
    pages = jnp.concatenate([key_rows, value_rows], axis=-1).reshape(
        -1, PAGE, kv_heads, 2 * head_dim
    )
    kv_pages = jnp.zeros_like(pages).at[page_table[0]].set(pages)
    token_index = jnp.arange(tok_count, dtype=jnp.int32)
    visible = (segment_row[None, :] == segment_row[:, None]) & (
        token_index[None, :] <= token_index[:, None]
    )
    local_scores = (
        jnp.einsum("tkgd,skd->kgts", grouped_query, key_rows, preferred_element_type=jnp.float32)
        * score_scale
    )
    local_scores = jnp.where(visible[None, None], local_scores, -jnp.inf)
    row_max = jnp.max(local_scores, axis=-1)
    numerators = jnp.exp(local_scores - row_max[..., None])
    totals = jnp.sum(numerators, axis=-1)
    weighted = jnp.einsum(
        "kgts,skd->kgtd",
        numerators.astype(jnp.bfloat16),
        value_rows,
        preferred_element_type=jnp.float32,
    )
    gathered = lax.all_gather(prefix_cache, "req", axis=0, tiled=True)
    window = tok_count // 2
    seg_count = prefix_group.shape[1]
    for seg in range(seg_count):
        start_row = jnp.minimum(jnp.sum((segment_row < seg).astype(jnp.int32)), tok_count - window)
        chosen = lax.dynamic_index_in_dim(gathered, prefix_group[0, seg], 0, keepdims=False)
        query_window = lax.dynamic_slice_in_dim(grouped_query, start_row, window, 0)
        scores = (
            jnp.einsum(
                "tkgd,skd->kgts",
                query_window,
                chosen[..., :head_dim],
                preferred_element_type=jnp.float32,
            )
            * score_scale
        )
        old_max = lax.dynamic_slice_in_dim(row_max, start_row, window, 2)
        old_total = lax.dynamic_slice_in_dim(totals, start_row, window, 2)
        old_weighted = lax.dynamic_slice_in_dim(weighted, start_row, window, 2)
        new_max = jnp.maximum(old_max, jnp.max(scores, axis=-1))
        decay_factor = jnp.exp(old_max - new_max)
        fresh = jnp.exp(scores - new_max[..., None])
        added = jnp.einsum(
            "kgts,skd->kgtd",
            fresh.astype(jnp.bfloat16),
            chosen[..., head_dim:],
            preferred_element_type=jnp.float32,
        )
        new_total = old_total * decay_factor + jnp.sum(fresh, axis=-1)
        new_weighted = old_weighted * decay_factor[..., None] + added
        inside = lax.dynamic_slice_in_dim(segment_row, start_row, window, 0) == seg
        row_max = lax.dynamic_update_slice_in_dim(
            row_max, jnp.where(inside[None, None], new_max, old_max), start_row, 2
        )
        totals = lax.dynamic_update_slice_in_dim(
            totals, jnp.where(inside[None, None], new_total, old_total), start_row, 2
        )
        weighted = lax.dynamic_update_slice_in_dim(
            weighted,
            jnp.where(inside[None, None, :, None], new_weighted, old_weighted),
            start_row,
            2,
        )
    attention = (
        (weighted / totals[..., None])
        .transpose(2, 0, 1, 3)
        .reshape(tok_count, -1)
        .astype(jnp.bfloat16)
    )
    partial_value = jnp.dot(attention, w_out, preferred_element_type=jnp.float32)
    share_width = hidden_in.shape[1]
    summed = lax.psum(partial_value.astype(jnp.bfloat16), "hid").astype(jnp.float32)
    middle = (whole.astype(jnp.float32) + summed).astype(jnp.bfloat16)
    middle_share = lax.dynamic_slice_in_dim(
        middle, lax.axis_index("hid") * share_width, share_width, 1
    )
    normed_moe = rms_scale(middle, moe_gain)
    local_experts = w_down.shape[0]
    experts = local_experts * req_count
    top_count = routes.shape[1]
    capacity = 2 * tok_count * top_count // experts
    flat_routes, slot = slots_of(routes, experts)
    target = flat_routes * capacity + slot
    token_rows = jnp.repeat(normed_moe, top_count, axis=0)
    outgoing = jnp.zeros((experts * capacity, model_width), jnp.bfloat16).at[target].set(token_rows)
    outgoing = outgoing.reshape(experts, capacity, model_width)
    partial_out = (lambda received: expert_rows(received, w_gate_up, w_down))(
        lax.all_to_all(outgoing, "req", split_axis=0, concat_axis=0, tiled=True)
    )
    reduced = lax.psum_scatter(
        partial_out.astype(jnp.bfloat16), "hid", scatter_dimension=2, tiled=True
    )
    returned = lax.all_to_all(reduced, "req", split_axis=0, concat_axis=0, tiled=True)
    picked = returned.reshape(experts * capacity, -1)[target].reshape(tok_count, top_count, -1)
    expert_sum = jnp.sum(picked.astype(jnp.float32) * gates[:, :, None], axis=1)
    hidden_out = (middle_share.astype(jnp.float32) + expert_sum).astype(jnp.bfloat16)
    return (hidden_out, kv_pages)


def solution(mesh):
    in_specs = (
        P("req", "hid"),
        P("req", None),
        P("req", None),
        P("req", None, "hid", None),
        P("req", None),
        P(),
        P(None, "hid"),
        P(None, "hid"),
        P("hid", None),
        P(),
        P("req", None),
        P("req", None),
        P("req", None, None, "hid"),
        P("req", "hid", None),
    )
    out_specs = (P("req", "hid"), P("req", None, "hid", None))
    return jax.shard_map(shards, mesh=mesh, in_specs=in_specs, out_specs=out_specs, check_vma=False)
```

profile of v0, /device:TPU:0, one launch (start us, length us, event | category | flops | bytes accessed | tf_op | source)
XLA Modules:
  0.0 529.4 jit_solution(13866989351808228242)
XLA Ops:
  7.3 2.5 copy.64
  28.5 4.5 reduce-window.6
  39.7 17.4 %all_gather.6 = bf16[256,1024]{1,0:T(8,128)(2,1)S(1)} all-gather(bf16[256,256]{1,0:T(8,128)(2,1)S(1)} %copy-done.8), channel_id=1, replica_groups=mesh['req'=8,'hid'=4] {'hid'}, dimensions={1}, use_global_device_ids=true | all-gather | bytes 655360 | tf_op jit(solution)/shard_map/all_gather | solution.py:81
  60.3 6.7 %all-gather.2.cloned.1.call-done = bf16[16,1024,2,128]{3,1,2,0:T(8,128)(2,1)} async-done(((bf16[2,1024,2,128]{3,1,2,0:T(8,128)(2,1)}), bf16[16,1024,2,128]{3,1,2,0:T(8,128)(2,1)}) %all-gather.2.cloned.1.call-update) | async-done | bytes 8388624 | tf_op jit(solution)/shard_map/all_gather | solution.py:124
  67.0 3.7 constant_dynamic-slice_fusion.8
  70.7 2.0 copy.79
  72.8 2.1 copy.77
  74.8 2.0 copy.75
  76.8 2.0 copy.73
  83.0 1.5 bitcast_reduce_fusion.7
  87.4 2.1 fusion.50
  89.5 1.2 dynamic_update_slice.71
  91.5 1.5 bitcast_reduce_fusion.6
  95.8 2.1 fusion.49
  97.9 1.8 dynamic_update_slice.73
  100.8 1.5 bitcast_reduce_fusion.5
  105.1 2.1 fusion.48
  107.2 1.8 dynamic_update_slice.75
  110.1 1.5 bitcast_reduce_fusion.4
  114.4 2.1 fusion.47
  116.4 1.8 dynamic_update_slice.77
  119.4 1.5 bitcast_reduce_fusion.3
  123.6 2.1 fusion.46
  125.7 1.8 dynamic_update_slice.79
  128.7 2.9 bitcast_reduce_fusion.2
  131.5 2.1 bitcast_reduce_fusion.1
  135.3 2.1 fusion.31
  137.5 1.4 add_select_fusion.2
  138.8 2.1 fusion.45
  140.9 1.8 dynamic_update_slice.81
  143.8 1.3 add_select_fusion.1
  146.1 2.1 fusion.44
  148.2 1.8 dynamic_update_slice.83
  151.1 1.6 bitcast_reduce_fusion
  155.7 38.7 %all-reduce.2.cloned.1.call-done = bf16[256,1024]{1,0:T(8,128)(2,1)} async-done(((bf16[256,1024]{1,0:T(8,128)(2,1)}), bf16[256,1024]{1,0:T(8,128)(2,1)}) %all-reduce.2.cloned.1.call-update) | async-done | bytes 524304 | tf_op jit(solution)/shard_map/psum | solution.py:175
  194.3 1.3 fusion.51
  196.6 14.6 %scatter_custom_fusion = bf16[4096,1024]{1,0:T(8,128)(2,1)} fusion(s32[2048]{0:T(1024)S(1)} %bitcast.369, bf16[]{:T(256)} %constant.98.clone.1, bf16[256,1024]{1,0:T(8,128)(2,1)S(1)} %fusion.53), kind=kCustom, calls=%fused_computation.8 | custom fusion | bytes 8912898 | tf_op jit(solution)/shard_map/scatter | solution.py:188
  211.2 98.2 %all_to_all.10 = bf16[16,256,1024]{2,1,0:T(8,128)(2,1)S(1)} all-to-all(bf16[16,256,1024]{2,1,0:T(8,128)(2,1)} %bitcast.321), channel_id=1, replica_groups=mesh['req'=8,'hid'=4] {'req'}, dimensions={0} | all-to-all | bytes 16777216 | tf_op jit(solution)/shard_map/all_to_all | solution.py:191
  309.4 3.2 copy-done.2
  312.6 3.7 fusion.2
  316.3 12.7 %convert_bitcast_fusion = bf16[8,2,256,1024]{3,2,0,1:T(8,128)(2,1)} fusion(f32[2,8,256,128]{3,2,1,0:T(8,128)} %fusion.2, bf16[8,2,256,1024]{3,2,1,0:T(8,128)(2,1)} %bitcast.323, bf16[2,128,1024]{2,1,0:T(8,128)(2,1)S(1)} %copy-done, bf16[2,2,1024,128]{3,2,1,0:T(8,128)(2,1)S(1)} %copy-done.35), kind=kOutput, calls=%fused_computation.3 | convolution fusion | flops 2154823680 | bytes 19922944 | tf_op jit(solution)/shard_map/recf,efd->recd/dot_general | solution.py:60
  329.0 7.9 %copy.88 = bf16[8,2,256,1024]{3,2,1,0:T(8,128)(2,1)} copy(bf16[8,2,256,1024]{3,2,0,1:T(8,128)(2,1)} %convert_bitcast_fusion) | data formatting | bytes 16777216 | tf_op jit(solution)/shard_map/convert_element_type | solution.py:194
  337.0 142.7 %reduce-scatter.2.cloned.1.call-done = bf16[16,256,256]{2,1,0:T(8,128)(2,1)} async-done(((bf16[16,256,1024]{2,1,0:T(8,128)(2,1)}), bf16[16,256,256]{2,1,0:T(8,128)(2,1)}) %reduce-scatter.2.cloned.1.call-update) | async-done | bytes 2097168 | tf_op jit(solution)/shard_map/reduce_scatter | solution.py:193
  479.7 3.7 all-to-all-start.1
  486.1 23.9 %all-to-all-done.1 = bf16[16,256,256]{2,1,0:T(8,128)(2,1)S(1)} async-done(((bf16[16,256,256]{2,1,0:T(8,128)(2,1)}), bf16[16,256,256]{2,1,0:T(8,128)(2,1)S(1)}, u32[]{:S(2)}, u32[]{:S(2)}) %all-to-all-start.1) | async-done | bytes 2097184 | tf_op jit(solution)/shard_map/all_to_all | solution.py:196
  509.9 9.0 %gather_fusion = bf16[2048,256]{1,0:T(8,128)(2,1)} fusion(bf16[4096,256]{1,0:T(8,128)(2,1)S(1)} %bitcast.319, s32[2048]{0:T(1024)S(1)} %broadcast_clamp_fusion), kind=kCustom, calls=%fused_computation | custom fusion | bytes 2105344 | tf_op jit(solution)/shard_map/gather | solution.py:197
  518.9 1.9 fusion.7
  520.9 1.6 add_convert_fusion
  (170 shorter events, 42.2 us)
Async XLA Ops:
  7.2 309.1 %copy-start = (bf16[2,128,1024]{2,1,0:T(8,128)(2,1)S(1)}, bf16[2,128,1024]{2,1,0:T(8,128)(2,1)}, u32[]{:S(2)}) copy-start(bf16[2,128,1024]{2,1,0:T(8,128)(2,1)} %param.27) | copy-start | bytes 1572868
  7.2 2.7 copy-start.17
  7.2 13.6 %copy-start.13 = (s32[1,256]{1,0:T(1,128)S(1)}, s32[1,256]{1,0:T(1,128)}, u32[]{:S(2)}) copy-start(s32[1,256]{1,0:T(1,128)} %param.15) | copy-start | bytes 3076
  7.2 19.5 %copy-start.16 = (s32[256,8]{0,1:T(8,128)S(1)}, s32[256,8]{0,1:T(8,128)}, u32[]{:S(2)}) copy-start(s32[256,8]{0,1:T(8,128)} %param.24) | copy-start | bytes 24580
  7.2 32.5 %copy-start.8 = (bf16[256,256]{1,0:T(8,128)(2,1)S(1)}, bf16[256,256]{1,0:T(8,128)(2,1)}, u32[]{:S(2)}) copy-start(bf16[256,256]{1,0:T(8,128)(2,1)} %param.14) | copy-start | bytes 393220
  7.2 59.8 %all-gather.2.cloned.1.call-start = ((), (), s32[]{:S(2)}) async-start(), calls=%async_computation.3 | async-start | bytes 9437184 | tf_op jit(solution)/shard_map/all_gather | solution.py:124
  9.8 47.8 %copy-start.36 = (bf16[1024,256]{1,0:T(8,128)(2,1)S(1)}, bf16[1024,256]{1,0:T(8,128)(2,1)}, u32[]{:S(2)}) copy-start(bf16[1024,256]{1,0:T(8,128)(2,1)} %param.21) | copy-start | bytes 1572868
  9.8 47.8 %copy-start.38 = (f32[1024]{0:T(1024)S(1)}, f32[1024]{0:T(1024)}, u32[]{:S(2)}) copy-start(f32[1024]{0:T(1024)} %param.19) | copy-start | bytes 12292
  9.8 184.5 %all-reduce.2.cloned.1.call-start = ((), (), s32[]{:S(2)}) async-start(), calls=%async_computation.4 | async-start | bytes 1048576 | tf_op jit(solution)/shard_map/psum | solution.py:175
  26.9 31.3 %copy-start.37 = (bf16[1024,256]{1,0:T(8,128)(2,1)S(1)}, bf16[1024,256]{1,0:T(8,128)(2,1)}, u32[]{:S(2)}) copy-start(bf16[1024,256]{1,0:T(8,128)(2,1)} %param.20) | copy-start | bytes 1572868
  39.6 44.9 %copy-start.29 = (pred[128]{0:T(512)(128)(4,1)}, pred[128]{0:T(512)(128)(4,1)S(1)}, u32[]{:S(2)}) copy-start(pred[128]{0:T(512)(128)(4,1)S(1)} %get-tuple-element.68) | copy-start | bytes 388
  58.1 1.9 copy-start.7
  58.1 1.1 copy-start.9
  58.1 1.1 copy-start.11
  85.2 0.6 copy-start.30
  89.5 3.5 copy-start.27
  91.5 2.6 copy-start.28
  97.9 4.4 copy-start.25
  100.8 2.6 copy-start.26
  107.2 4.4 copy-start.23
  110.1 2.6 copy-start.24
  116.4 4.4 copy-start.21
  119.3 2.6 copy-start.22
  128.7 5.0 copy-start.20
  134.3 3.2 copy-start.18
  135.3 2.1 copy-start.19
  135.3 3.5 copy-start.1
  138.8 3.9 copy-start.32
  151.1 2.1 copy-start.33
  151.1 2.1 copy-start.4
  153.1 1.2 copy-start.5
  153.2 2.3 copy-start.6
  153.3 2.3 copy-start.14
  153.3 2.4 copy-start.15
  153.8 42.7 %copy-start.34 = (f32[1024]{0:T(1024)S(1)}, f32[1024]{0:T(1024)}, u32[]{:S(2)}) copy-start(f32[1024]{0:T(1024)} %param.23) | copy-start | bytes 12292
  155.5 324.2 %reduce-scatter.2.cloned.1.call-start = ((), (), s32[]{:S(2)}) async-start(), calls=%async_computation.5 | async-start | bytes 10485760 | tf_op jit(solution)/shard_map/reduce_scatter | solution.py:193
  195.6 0.8 copy-start.3
  211.2 101.4 %copy-start.35 = (bf16[2,2,1024,128]{3,2,1,0:T(8,128)(2,1)S(1)}, bf16[2,2,1024,128]{3,2,1,0:T(8,128)(2,1)}, u32[]{:S(2)}) copy-start(bf16[2,2,1024,128]{3,2,1,0:T(8,128)(2,1)} %param.26) | copy-start | bytes 3145732
  309.4 3.2 copy-start.2
  336.9 147.3 %copy-start.31 = (f32[256,8]{0,1:T(8,128)S(1)}, f32[256,8]{0,1:T(8,128)}, u32[]{:S(2)}) copy-start(f32[256,8]{0,1:T(8,128)} %param.25) | copy-start | bytes 24580
  336.9 147.4 %copy-start.10 = (bf16[256,2,32]{0,2,1:T(8,128)(2,1)S(1)}, bf16[256,2,32]{0,2,1:T(8,128)(2,1)}, u32[]{:S(2)}) copy-start(bf16[256,2,32]{0,2,1:T(8,128)(2,1)} %copy-done.9) | copy-start | bytes 98308
  336.9 147.4 %copy-start.12 = (bf16[256,2,32]{0,2,1:T(8,128)(2,1)S(1)}, bf16[256,2,32]{0,2,1:T(8,128)(2,1)}, u32[]{:S(2)}) copy-start(bf16[256,2,32]{0,2,1:T(8,128)(2,1)} %copy-done.11) | copy-start | bytes 98308
  337.0 147.6 %copy-start.39 = (s32[1,2]{1,0:T(1,128)S(1)}, s32[1,2]{1,0:T(1,128)}, u32[]{:S(2)}) copy-start(s32[1,2]{1,0:T(1,128)} %param.18) | copy-start | bytes 28
  479.7 30.3 %all-to-all-start.1 = ((bf16[16,256,256]{2,1,0:T(8,128)(2,1)}), bf16[16,256,256]{2,1,0:T(8,128)(2,1)S(1)}, u32[]{:S(2)}, u32[]{:S(2)}) async-start(bf16[16,256,256]{2,1,0:T(8,128)(2,1)} %reduce-scatter.2.cloned.1.call-done), calls=%async_computation.2 | async-start | bytes 4194304 | tf_op jit(solution)/shard_map/all_to_all | solution.py:196
Sparse Core Ops, SparseCore 0:
  9.9 57.0 all-gather.1
  155.6 38.6 all-reduce.1
  337.0 142.5 reduce-scatter.1
where the time goes:
time: 536 us; the launch traced here: 529 us
  waiting for transfers between devices  212 us (40%)
  blocking collectives  116 us (22%)
  local copies, waits for them, and re-layouts  86.5 us (16%)
  matrix products  48.3 us (9%)
  between operations  35.6 us (7%)
  other arithmetic  27.8 us (5%)
    reduce_scatter x1, waiting for transfers between devices, shards(): lax.psum_scatter(partial_out.astype(jnp.bfloat16), 'hid', scatter_dimensi...  143 us
    all_to_all x1, blocking collectives, shards(): lax.all_to_all(outgoing, 'req', split_axis=0, concat_axis=0, tiled=True)  98.2 us
    psum x1, waiting for transfers between devices, shards(): lax.psum(partial_value.astype(jnp.bfloat16), 'hid').astype(jnp.float32)  38.7 us
    all_to_all x1, waiting for transfers between devices, shards(): lax.all_to_all(reduced, 'req', split_axis=0, concat_axis=0, tiled=True)  23.9 us
    all_gather x1, blocking collectives, shards(): whole = lax.all_gather(hidden_in, 'hid', axis=1, tiled=True)  17.4 us
    dynamic_slice x9, local copies, waits for them, and re-layouts, shards(): lax.dynamic_index_in_dim(gathered, prefix_group[0, seg], 0, keepdims=False)  16 us
    dot_general x8, matrix products, shards(): jnp.einsum('kgts,skd->kgtd', fresh.astype(jnp.bfloat16), chosen[..., head...  15.1 us
    scatter x1, local copies, waits for them, and re-layouts, shards(): jnp.zeros((experts * capacity, model_width), jnp.bfloat16).at[target]  14.6 us
  transfers between devices with their start and end apart: 4, of which 4 were waited for; matrix products, arithmetic and copies ran while one was open for 3% of the time, Pallas kernels for 0%

commit v1 on v0

--- a/solution.py
+++ b/solution.py
@@ -170,32 +170,35 @@
         .reshape(tok_count, -1)
         .astype(jnp.bfloat16)
     )
-    partial_value = jnp.dot(attention, w_out, preferred_element_type=jnp.float32)
     share_width = hidden_in.shape[1]
-    summed = lax.psum(partial_value.astype(jnp.bfloat16), "hid").astype(jnp.float32)
-    middle = (whole.astype(jnp.float32) + summed).astype(jnp.bfloat16)
+    whole_attention = lax.all_gather(attention, "hid", axis=1, tiled=True)
+    whole_w_out = lax.all_gather(w_out, "hid", axis=0, tiled=True)
+    projected_out = jnp.dot(whole_attention, whole_w_out, preferred_element_type=jnp.float32)
+    middle = (whole.astype(jnp.float32) + projected_out).astype(jnp.bfloat16)
     middle_share = lax.dynamic_slice_in_dim(
         middle, lax.axis_index("hid") * share_width, share_width, 1
     )
     normed_moe = rms_scale(middle, moe_gain)
-    local_experts = w_down.shape[0]
-    experts = local_experts * req_count
-    top_count = routes.shape[1]
-    capacity = 2 * tok_count * top_count // experts
-    flat_routes, slot = slots_of(routes, experts)
-    target = flat_routes * capacity + slot
-    token_rows = jnp.repeat(normed_moe, top_count, axis=0)
-    outgoing = jnp.zeros((experts * capacity, model_width), jnp.bfloat16).at[target].set(token_rows)
-    outgoing = outgoing.reshape(experts, capacity, model_width)
-    partial_out = (lambda received: expert_rows(received, w_gate_up, w_down))(
-        lax.all_to_all(outgoing, "req", split_axis=0, concat_axis=0, tiled=True)
-    )
-    reduced = lax.psum_scatter(
-        partial_out.astype(jnp.bfloat16), "hid", scatter_dimension=2, tiled=True
-    )
-    returned = lax.all_to_all(reduced, "req", split_axis=0, concat_axis=0, tiled=True)
-    picked = returned.reshape(experts * capacity, -1)[target].reshape(tok_count, top_count, -1)
-    expert_sum = jnp.sum(picked.astype(jnp.float32) * gates[:, :, None], axis=1)
+    all_gate_up = lax.all_gather(w_gate_up, "req", axis=0, tiled=True)
+    all_down = lax.all_gather(w_down, "req", axis=0, tiled=True)
+    experts = all_down.shape[0]
+    expert_ids = jnp.arange(experts, dtype=jnp.int32)
+    combine = jnp.sum(
+        jnp.where(routes[:, :, None] == expert_ids[None, None, :], gates[:, :, None], 0.0), axis=1
+    )
+    gate_proj = jnp.einsum(
+        "td,edf->tef", normed_moe, all_gate_up[:, 0], preferred_element_type=jnp.float32
+    )
+    up_proj = jnp.einsum(
+        "td,edf->tef", normed_moe, all_gate_up[:, 1], preferred_element_type=jnp.float32
+    )
+    hidden = (jax.nn.silu(gate_proj) * up_proj * combine[:, :, None]).astype(jnp.bfloat16)
+    partial_out = jnp.einsum(
+        "tef,efd->td", hidden, all_down, preferred_element_type=jnp.float32
+    )
+    expert_sum = lax.psum_scatter(
+        partial_out.astype(jnp.bfloat16), "hid", scatter_dimension=1, tiled=True
+    ).astype(jnp.float32)
     hidden_out = (middle_share.astype(jnp.float32) + expert_sum).astype(jnp.bfloat16)
     return (hidden_out, kv_pages)
 

time: 536 us -> 247 us (0.46)
  waiting for transfers between devices: 212 us -> 66 us
  blocking collectives: 116 us -> 33.3 us
  local copies, waits for them, and re-layouts: 86.5 us -> 50.5 us
  other arithmetic: 27.8 us -> 18.3 us
  matrix products: 48.3 us -> 42.4 us
    reduce_scatter x1, waiting for transfers between devices: 143 us -> 19.4 us  [shards(): lax.psum_scatter(partial_out.astype(jnp.bfloat16), 'hid', scatter_dimensi...]
    all_to_all x1 -> x0, blocking collectives: 98.2 us -> none  [shards(): lax.all_to_all(outgoing, 'req', split_axis=0, concat_axis=0, tiled=True)]
    psum x1 -> x0, waiting for transfers between devices: 38.7 us -> none  [shards(): lax.psum(partial_value.astype(jnp.bfloat16), 'hid').astype(jnp.float32)]
    all_gather x0 -> x3, waiting for transfers between devices: none -> 33.5 us  [the longest x1 33.4 us: shards(): all_down = lax.all_gather(w_down, 'req', axis=0, tiled=True)]
    all_to_all x1 -> x0, waiting for transfers between devices: 23.9 us -> none  [shards(): lax.all_to_all(reduced, 'req', split_axis=0, concat_axis=0, tiled=True)]
    all_gather x0 -> x1, blocking collectives: none -> 15.9 us  [shards(): whole_attention = lax.all_gather(attention, 'hid', axis=1, tiled=True)]
    scatter x1 -> x0, local copies, waits for them, and re-layouts: 14.6 us -> none  [shards(): jnp.zeros((experts * capacity, model_width), jnp.bfloat16).at[target]]
    gather x1 -> x0, local copies, waits for them, and re-layouts: 9 us -> none  [shards(): returned.reshape(experts * capacity, -1)[target]]
  transfers between devices with their start and end apart: 4 -> 5, of which waited for: 4 -> 4; matrix products, arithmetic and copies ran while one was open for 3% -> 40% of each run, Pallas kernels for 0% -> 0%
where the time goes in v1:
time: 247 us; the launch traced here: 245 us
  waiting for transfers between devices  66 us (27%)
  local copies, waits for them, and re-layouts  50.5 us (20%)
  matrix products  42.4 us (17%)
  between operations  34.4 us (14%)
  blocking collectives  33.3 us (13%)
  other arithmetic  18.3 us (7%)
    all_gather x1, waiting for transfers between devices, shards(): all_down = lax.all_gather(w_down, 'req', axis=0, tiled=True)  33.4 us
    reduce_scatter x1, waiting for transfers between devices, shards(): lax.psum_scatter(partial_out.astype(jnp.bfloat16), 'hid', scatter_dimensi...  19.4 us
    all_gather x1, blocking collectives, shards(): whole = lax.all_gather(hidden_in, 'hid', axis=1, tiled=True)  17.4 us
    dynamic_slice x9, local copies, waits for them, and re-layouts, shards(): lax.dynamic_index_in_dim(gathered, prefix_group[0, seg], 0, keepdims=False)  16.1 us
    all_gather x1, blocking collectives, shards(): whole_attention = lax.all_gather(attention, 'hid', axis=1, tiled=True)  15.9 us
    dot_general x8, matrix products, shards(): jnp.einsum('kgts,skd->kgtd', fresh.astype(jnp.bfloat16), chosen[..., head...  14.9 us
    dynamic_update_slice x8, local copies, waits for them, and re-layouts, shards(): lax.dynamic_update_slice_in_dim(weighted, jnp.where(inside[None, None, :,...  12.5 us
    all_gather x1, waiting for transfers between devices, shards(): gathered = lax.all_gather(prefix_cache, 'req', axis=0, tiled=True)  11.8 us
  transfers between devices with their start and end apart: 5, of which 4 were waited for; matrix products, arithmetic and copies ran while one was open for 40% of the time, Pallas kernels for 0%

profile of v1, /device:TPU:0, one launch (start us, length us, event | category | flops | bytes accessed | tf_op | source)
XLA Modules:
  0.0 245.1 jit_solution(16315428064738042846)
XLA Ops:
  7.2 2.4 copy.62
  10.6 1.1 copy.79
  29.0 17.4 %all_gather.18 = bf16[256,1024]{1,0:T(8,128)(2,1)S(1)} all-gather(bf16[256,256]{1,0:T(8,128)(2,1)S(1)} %copy-done.8), channel_id=1, replica_groups=mesh['req'=8,'hid'=4] {'hid'}, dimensions={1}, use_global_device_ids=true | all-gather | bytes 655360 | tf_op jit(solution)/shard_map/all_gather | solution.py:81
  55.1 11.8 %all-gather.5.cloned.1.call-done = bf16[16,1024,2,128]{3,1,2,0:T(8,128)(2,1)} async-done(((bf16[2,1024,2,128]{3,1,2,0:T(8,128)(2,1)}), bf16[16,1024,2,128]{3,1,2,0:T(8,128)(2,1)}) %all-gather.5.cloned.1.call-update) | async-done | bytes 8388624 | tf_op jit(solution)/shard_map/all_gather | solution.py:124
  67.0 3.6 %constant_dynamic-slice_fusion.8 = (bf16[1,1024,2,128]{3,1,2,0:T(8,128)(2,1)}, bf16[1,1024,2,128]{3,1,2,0:T(8,128)(2,1)}, bf16[1,1024,2,128]{3,1,2,0:T(8,128)(2,...) fusion(bf16[16,1024,2,128]{3,1,2,0:T(8,128)(2,1)} %all-gather.5, ...), kind=kLoop, calls=%fused_computation.182 | loop fusion | bytes 8388640 | tf_op jit(solution)/shard_map/jit(dynamic_index_in_dim)/dynamic_slice | solution.py:129
  70.6 2.1 copy.77
  72.7 2.1 copy.75
  74.7 2.1 copy.73
  76.8 2.1 copy.71
  78.9 1.1 copy.69
  83.0 1.5 bitcast_reduce_fusion.7
  87.4 2.1 fusion.37
  89.5 1.2 dynamic_update_slice.71
  91.5 1.5 bitcast_reduce_fusion.6
  95.8 2.1 fusion.36
  97.9 1.8 dynamic_update_slice.73
  99.7 1.0 dynamic_update_slice.87
  100.8 1.5 bitcast_reduce_fusion.5
  104.0 1.0 dynamic_update_slice.76
  105.0 2.1 fusion.35
  107.1 1.8 dynamic_update_slice.75
  109.9 1.5 bitcast_reduce_fusion.4
  114.2 2.1 fusion.34
  116.3 1.8 dynamic_update_slice.77
  118.2 1.1 dynamic_update_slice.89
  119.2 1.5 bitcast_reduce_fusion.3
  122.5 1.0 dynamic_update_slice.80
  123.5 2.1 fusion.33
  125.6 1.8 dynamic_update_slice.79
  127.5 1.0 dynamic_update_slice.90
  128.5 1.5 bitcast_reduce_fusion.2
  130.1 1.3 broadcast_select_fusion.1
  131.4 1.0 dynamic_update_slice.82
  134.1 1.4 add_select_fusion.2
  135.5 1.8 fusion.32
  137.3 1.8 dynamic_update_slice.81
  140.2 1.3 add_select_fusion.1
  142.5 2.2 fusion.31
  144.7 1.8 dynamic_update_slice.83
  146.5 1.0 dynamic_update_slice.92
  147.6 1.6 bitcast_reduce_fusion
  150.8 15.9 %all_gather.20 = bf16[256,1024]{0,1:T(8,128)(2,1)S(1)} all-gather(bf16[256,256]{0,1:T(8,128)(2,1)S(1)} %bitcast.297), channel_id=1, replica_groups=mesh['req'=8,'hid'=4] {'hid'}, dimensions={1}, use_global_device_ids=true | all-gather | bytes 655360 | tf_op jit(solution)/shard_map/all_gather | solution.py:174
  166.7 2.4 fusion.38
  169.2 4.9 %fusion.1 = f32[256,16,128]{2,0,1:T(8,128)} fusion(bf16[16,2,1024,128]{3,2,0,1:T(8,128)(2,1)} %all-gather.9.cloned.1.call-done, bf16[256,1024]{1,0:T(8,128)(2,1)S(1)} %get-tuple-element.95, f32[1024]{0:T(1024)S(1)} %copy-done.35, f32[256]{0:T(256)S(1)} %add_rsqrt_fusion), kind=kOutput, calls=%fused_computation.4 | convolution fusion | flops 1074790400 | bytes 6820864 | tf_op jit(solution)/shard_map/td,edf->tef/dot_general | solution.py:189
  174.1 33.4 %all-gather.11.cloned.1.call-done = bf16[16,128,1024]{2,1,0:T(8,128)(2,1)} async-done(((bf16[2,128,1024]{2,1,0:T(8,128)(2,1)}), bf16[16,128,1024]{2,1,0:T(8,128)(2,1)}) %all-gather.11.cloned.1.call-update) | async-done | bytes 4194320 | tf_op jit(solution)/shard_map/all_gather | solution.py:183
  207.6 7.3 %fusion.29 = bf16[256,1024]{1,0:T(8,128)(2,1)} fusion(bf16[16,128,1024]{2,1,0:T(8,128)(2,1)} %all-gather.11.cloned.1.call-done, f32[256,16,128]{2,0,1:T(8,128)} %fusion.1, bf16[16,2,1024,128]{3,2,0,1:T(8,128)(2,1)} %all-gather.9.cloned.1.call-done, f32[256,16]{0,1:T(8,128)S(1)} %copy-done.16, bf16[256,1024]{1,0:T(8,128)(2,1)S(1)} %get-tuple-element.95, ...), kind=kOutput, calls=%fused_computation.56 | convolution fusion | flops 2152464384 | bytes 11555840 | tf_op jit(solution)/shard_map/tef,efd->td/dot_general | solution.py:196
  217.5 19.4 %reduce-scatter.2.cloned.1.call-done = bf16[256,256]{1,0:T(8,128)(2,1)} async-done(((bf16[256,1024]{1,0:T(8,128)(2,1)}), bf16[256,256]{1,0:T(8,128)(2,1)}) %reduce-scatter.2.cloned.1.call-update) | async-done | bytes 131088 | tf_op jit(solution)/shard_map/reduce_scatter | solution.py:199
  236.9 1.6 add_convert_fusion
  (149 shorter events, 31.2 us)
Async XLA Ops:
  7.2 39.4 %copy-start = (bf16[1024,256]{1,0:T(8,128)(2,1)S(1)}, bf16[1024,256]{1,0:T(8,128)(2,1)}, u32[]{:S(2)}) copy-start(bf16[1024,256]{1,0:T(8,128)(2,1)} %param.20) | copy-start | bytes 1572868
  7.2 3.4 %copy-start.6 = (bf16[2,2,1024,128]{3,2,1,0:T(8,128)(2,1)S(1)}, bf16[2,2,1024,128]{3,2,1,0:T(8,128)(2,1)}, u32[]{:S(2)}) copy-start(bf16[2,2,1024,128]{3,2,1,0:T(8,128)(2,1)} %param.26) | copy-start | bytes 3145732
  7.2 59.8 %all-gather.5.cloned.1.call-start = ((), (), s32[]{:S(2)}) async-start(), calls=%async_computation.1 | async-start | bytes 9437184 | tf_op jit(solution)/shard_map/all_gather | solution.py:124
  9.7 2.6 %copy-start.14 = (s32[1,8]{1,0:T(1,128)S(1)}, s32[1,8]{1,0:T(1,128)}, u32[]{:S(2)}) copy-start(s32[1,8]{1,0:T(1,128)} %param.16) | copy-start | bytes 100
  9.7 13.0 %copy-start.13 = (s32[1,256]{1,0:T(1,128)S(1)}, s32[1,256]{1,0:T(1,128)}, u32[]{:S(2)}) copy-start(s32[1,256]{1,0:T(1,128)} %param.15) | copy-start | bytes 3076
  9.7 19.3 %copy-start.8 = (bf16[256,256]{1,0:T(8,128)(2,1)S(1)}, bf16[256,256]{1,0:T(8,128)(2,1)}, u32[]{:S(2)}) copy-start(bf16[256,256]{1,0:T(8,128)(2,1)} %param.14) | copy-start | bytes 393220
  9.7 156.9 %all-gather.7.cloned.1.call-start = ((), (), s32[]{:S(2)}) async-start(), calls=%async_computation.2 | async-start | bytes 2621440 | tf_op jit(solution)/shard_map/all_gather | solution.py:175
  10.5 36.1 %copy-start.34 = (f32[1024]{0:T(1024)S(1)}, f32[1024]{0:T(1024)}, u32[]{:S(2)}) copy-start(f32[1024]{0:T(1024)} %param.19) | copy-start | bytes 12292
  10.5 158.7 %all-gather.9.cloned.1.call-start = ((), (), s32[]{:S(2)}) async-start(), calls=%async_computation.3 | async-start | bytes 9437184 | tf_op jit(solution)/shard_map/all_gather | solution.py:182
  11.6 35.4 %copy-start.33 = (bf16[1024,256]{1,0:T(8,128)(2,1)S(1)}, bf16[1024,256]{1,0:T(8,128)(2,1)}, u32[]{:S(2)}) copy-start(bf16[1024,256]{1,0:T(8,128)(2,1)} %param.21) | copy-start | bytes 1572868
  11.7 195.9 %all-gather.11.cloned.1.call-start = ((), (), s32[]{:S(2)}) async-start(), calls=%async_computation.4 | async-start | bytes 4718592 | tf_op jit(solution)/shard_map/all_gather | solution.py:183
  12.2 224.7 %reduce-scatter.2.cloned.1.call-start = ((), (), s32[]{:S(2)}) async-start(), calls=%async_computation.5 | async-start | bytes 655360 | tf_op jit(solution)/shard_map/reduce_scatter | solution.py:199
  47.5 0.7 copy-start.7
  47.8 6.1 %copy-start.29 = (f32[256,8]{0,1:T(8,128)S(1)}, f32[256,8]{0,1:T(8,128)}, u32[]{:S(2)}) copy-start(f32[256,8]{0,1:T(8,128)} %param.25) | copy-start | bytes 24580
  47.8 6.1 %copy-start.30 = (s32[256,8]{0,1:T(8,128)S(1)}, s32[256,8]{0,1:T(8,128)}, u32[]{:S(2)}) copy-start(s32[256,8]{0,1:T(8,128)} %param.24) | copy-start | bytes 24580
  47.8 0.6 copy-start.9
  47.8 0.6 copy-start.11
  55.1 29.4 %copy-start.27 = (pred[128]{0:T(512)(128)(4,1)}, pred[128]{0:T(512)(128)(4,1)S(1)}, u32[]{:S(2)}) copy-start(pred[128]{0:T(512)(128)(4,1)S(1)} %get-tuple-element.66) | copy-start | bytes 388
  85.2 0.7 copy-start.28
  89.5 3.5 %copy-start.25 = (pred[128]{0:T(512)(128)(4,1)S(1)}, pred[128]{0:T(512)(128)(4,1)}, u32[]{:S(2)}) copy-start(pred[128]{0:T(512)(128)(4,1)} %get-tuple-element.65) | copy-start | bytes 388
  91.5 2.6 %copy-start.26 = (pred[128]{0:T(512)(128)(4,1)S(1)}, pred[128]{0:T(512)(128)(4,1)}, u32[]{:S(2)}) copy-start(pred[128]{0:T(512)(128)(4,1)} %get-tuple-element.65) | copy-start | bytes 388
  97.9 4.4 %copy-start.23 = (pred[128]{0:T(512)(128)(4,1)S(1)}, pred[128]{0:T(512)(128)(4,1)}, u32[]{:S(2)}) copy-start(pred[128]{0:T(512)(128)(4,1)} %get-tuple-element.64) | copy-start | bytes 388
  100.8 2.6 %copy-start.24 = (pred[128]{0:T(512)(128)(4,1)S(1)}, pred[128]{0:T(512)(128)(4,1)}, u32[]{:S(2)}) copy-start(pred[128]{0:T(512)(128)(4,1)} %get-tuple-element.64) | copy-start | bytes 388
  107.1 4.4 %copy-start.21 = (pred[128]{0:T(512)(128)(4,1)S(1)}, pred[128]{0:T(512)(128)(4,1)}, u32[]{:S(2)}) copy-start(pred[128]{0:T(512)(128)(4,1)} %get-tuple-element.63) | copy-start | bytes 388
  109.9 2.6 %copy-start.22 = (pred[128]{0:T(512)(128)(4,1)S(1)}, pred[128]{0:T(512)(128)(4,1)}, u32[]{:S(2)}) copy-start(pred[128]{0:T(512)(128)(4,1)} %get-tuple-element.63) | copy-start | bytes 388
  116.3 4.4 %copy-start.19 = (pred[128]{0:T(512)(128)(4,1)S(1)}, pred[128]{0:T(512)(128)(4,1)}, u32[]{:S(2)}) copy-start(pred[128]{0:T(512)(128)(4,1)} %get-tuple-element.62) | copy-start | bytes 388
  119.2 2.6 %copy-start.20 = (pred[128]{0:T(512)(128)(4,1)S(1)}, pred[128]{0:T(512)(128)(4,1)}, u32[]{:S(2)}) copy-start(pred[128]{0:T(512)(128)(4,1)} %get-tuple-element.62) | copy-start | bytes 388
  130.1 2.8 %copy-start.1 = (f32[2,1024,128,2]{2,1,3,0:T(8,128)}, f32[2,1024,128,2]{2,1,3,0:T(8,128)S(1)}, u32[]{:S(2)}) copy-start(f32[2,1024,128,2]{2,1,3,0:T(8,128)S(1)} %get-tuple-element.89) | copy-start | bytes 6291460
  131.4 2.6 %copy-start.15 = (f32[2,2,128]{2,1,0:T(2,128)}, f32[2,2,128]{2,1,0:T(2,128)S(1)}, u32[]{:S(2)}) copy-start(f32[2,2,128]{2,1,0:T(2,128)S(1)} %get-tuple-element.35) | copy-start | bytes 6148
  132.5 1.0 copy-start.4
  132.5 1.6 copy-start.17
  132.5 1.6 copy-start.18
  132.5 3.0 %copy-start.5 = (bf16[1,1024,2,128]{1,3,2,0:T(8,128)(2,1)S(1)}, bf16[1,1024,2,128]{1,3,2,0:T(8,128)(2,1)}, u32[]{:S(2)}) copy-start(bf16[1,1024,2,128]{1,3,2,0:T(8,128)(2,1)} %copy.73) | copy-start | bytes 1572868
  133.5 2.0 copy-start.2
  135.5 3.7 %copy-start.31 = (f32[2,2,128]{2,1,0:T(2,128)S(1)}, f32[2,2,128]{2,1,0:T(2,128)}, u32[]{:S(2)}) copy-start(f32[2,2,128]{2,1,0:T(2,128)} %get-tuple-element.20) | copy-start | bytes 6148
  147.5 2.0 copy-start.32
  147.6 2.1 copy-start.3
  150.7 18.5 %copy-start.35 = (f32[1024]{0:T(1024)S(1)}, f32[1024]{0:T(1024)}, u32[]{:S(2)}) copy-start(f32[1024]{0:T(1024)} %param.23) | copy-start | bytes 12292
  169.2 38.4 %copy-start.16 = (f32[256,16]{0,1:T(8,128)S(1)}, f32[256,16]{0,1:T(8,128)}, u32[]{:S(2)}) copy-start(f32[256,16]{0,1:T(8,128)} %select_reduce_fusion) | copy-start | bytes 49156
  174.1 41.7 %copy-start.10 = (bf16[256,2,32]{0,2,1:T(8,128)(2,1)S(1)}, bf16[256,2,32]{0,2,1:T(8,128)(2,1)}, u32[]{:S(2)}) copy-start(bf16[256,2,32]{0,2,1:T(8,128)(2,1)} %copy-done.9) | copy-start | bytes 98308
  174.1 41.7 %copy-start.12 = (bf16[256,2,32]{0,2,1:T(8,128)(2,1)S(1)}, bf16[256,2,32]{0,2,1:T(8,128)(2,1)}, u32[]{:S(2)}) copy-start(bf16[256,2,32]{0,2,1:T(8,128)(2,1)} %copy-done.11) | copy-start | bytes 98308
  174.1 41.9 %copy-start.36 = (s32[1,2]{1,0:T(1,128)S(1)}, s32[1,2]{1,0:T(1,128)}, u32[]{:S(2)}) copy-start(s32[1,2]{1,0:T(1,128)} %param.18) | copy-start | bytes 28
Sparse Core Ops, SparseCore 0:
  9.9 57.0 all-gather.4
  68.5 45.6 all-gather.6
  116.2 53.0 all-gather.8
  171.0 36.5 all-gather.10
  215.0 21.8 reduce-scatter.1

commit v2 on v1

--- a/solution.py
+++ b/solution.py
@@ -59,6 +59,23 @@
     hidden = (jax.nn.silu(gate_proj) * up_proj).astype(jnp.bfloat16)
     produced = jnp.einsum("recf,efd->recd", hidden, down_proj, preferred_element_type=jnp.float32)
     return produced.reshape(-1, slot_count, model_width)
+
+
+def shifted_copies(block, axis_name):
+    count = lax.axis_size(axis_name)
+    copies = [block]
+    for shift in range(1, count):
+        pairs = [(index, (index + shift) % count) for index in range(count)]
+        copies.append(lax.ppermute(block, axis_name, pairs))
+    return copies
+
+
+def gather_in_order(block, axis_name, axis):
+    count = lax.axis_size(axis_name)
+    copies = jnp.stack(shifted_copies(block, axis_name))
+    order = (lax.axis_index(axis_name) - jnp.arange(count, dtype=jnp.int32)) % count
+    picked = jnp.take(copies, order, axis=0)
+    return jnp.concatenate([picked[index] for index in range(count)], axis=axis)
 
 
 def shards(
@@ -78,7 +95,7 @@
     w_down,
 ):
     req_count = lax.axis_size("req")
-    whole = lax.all_gather(hidden_in, "hid", axis=1, tiled=True)
+    whole = gather_in_order(hidden_in, "hid", 1)
     tok_count = whole.shape[0]
     model_width = whole.shape[1]
     segment_row = segments[0]
@@ -171,8 +188,8 @@
         .astype(jnp.bfloat16)
     )
     share_width = hidden_in.shape[1]
-    whole_attention = lax.all_gather(attention, "hid", axis=1, tiled=True)
-    whole_w_out = lax.all_gather(w_out, "hid", axis=0, tiled=True)
+    whole_attention = jnp.concatenate(shifted_copies(attention, "hid"), axis=1)
+    whole_w_out = jnp.concatenate(shifted_copies(w_out, "hid"), axis=0)
     projected_out = jnp.dot(whole_attention, whole_w_out, preferred_element_type=jnp.float32)
     middle = (whole.astype(jnp.float32) + projected_out).astype(jnp.bfloat16)
     middle_share = lax.dynamic_slice_in_dim(
@@ -180,8 +197,13 @@
     )
     normed_moe = rms_scale(middle, moe_gain)
     all_gate_up = lax.all_gather(w_gate_up, "req", axis=0, tiled=True)
-    all_down = lax.all_gather(w_down, "req", axis=0, tiled=True)
+    local_experts = w_down.shape[0]
+    all_down = jnp.concatenate(shifted_copies(w_down, "req"), axis=0)
     experts = all_down.shape[0]
+    down_ids = (
+        (lax.axis_index("req") - jnp.arange(req_count, dtype=jnp.int32)[:, None]) % req_count
+    ) * local_experts + jnp.arange(local_experts, dtype=jnp.int32)[None, :]
+    order = down_ids.reshape(-1)
     expert_ids = jnp.arange(experts, dtype=jnp.int32)
     combine = jnp.sum(
         jnp.where(routes[:, :, None] == expert_ids[None, None, :], gates[:, :, None], 0.0), axis=1
@@ -194,7 +216,7 @@
     )
     hidden = (jax.nn.silu(gate_proj) * up_proj * combine[:, :, None]).astype(jnp.bfloat16)
     partial_out = jnp.einsum(
-        "tef,efd->td", hidden, all_down, preferred_element_type=jnp.float32
+        "tef,efd->td", jnp.take(hidden, order, axis=1), all_down, preferred_element_type=jnp.float32
     )
     expert_sum = lax.psum_scatter(
         partial_out.astype(jnp.bfloat16), "hid", scatter_dimension=1, tiled=True

time: 247 us -> 225 us (0.911)
  blocking collectives: 33.3 us -> 0 us
  starting transfers between devices: 0.2 us -> 21.5 us
  matrix products: 42.4 us -> 35.8 us
  waiting for transfers between devices: 66 us -> 61.4 us
  local copies, waits for them, and re-layouts: 50.5 us -> 53.5 us
  other arithmetic: 18.3 us -> 15.8 us
    ppermute x0 -> x16, waiting for transfers between devices: none -> 42.9 us  [shifted_copies(): copies.append(lax.ppermute(block, axis_name, pairs))]
    all_gather x2 -> x0, waiting for transfers between devices: 33.4 us -> none  [the longest x1 33.4 us: shards(): all_down = lax.all_gather(w_down, 'req', axis=0, tiled=True)]
    all_gather x2 -> x0, blocking collectives: 33.3 us -> none  [the longest x1 17.4 us: shards(): whole = lax.all_gather(hidden_in, 'hid', axis=1, tiled=True)]
    ppermute x0 -> x16, starting transfers between devices: none -> 21.4 us  [shifted_copies(): copies.append(lax.ppermute(block, axis_name, pairs))]
    all_gather x1, waiting for transfers between devices: 11.8 us -> 0.01 us  [shards(): gathered = lax.all_gather(prefix_cache, 'req', axis=0, tiled=True)]
    unnamed x78 -> x105, local copies, waits for them, and re-layouts: 5.65 us -> 17.3 us
    dynamic_update_slice x8, local copies, waits for them, and re-layouts: 12.5 us -> 6.07 us  [shards(): lax.dynamic_update_slice_in_dim(weighted, jnp.where(inside[None, None, :,...]
    dynamic_update_slice x7, local copies, waits for them, and re-layouts: 7 us -> 2.67 us  [shards(): lax.dynamic_update_slice_in_dim(row_max, jnp.where(inside[None, None], ne...]
  transfers between devices with their start and end apart: 5 -> 19, of which waited for: 4 -> 3; matrix products, arithmetic and copies ran while one was open for 40% -> 39% of each run, Pallas kernels for 0% -> 0%
where the time goes in v2:
time: 225 us; the launch traced here: 223 us
  waiting for transfers between devices  61.4 us (27%)
  local copies, waits for them, and re-layouts  53.5 us (24%)
  matrix products  35.8 us (16%)
  between operations  35.3 us (16%)
  starting transfers between devices  21.5 us (10%)
  other arithmetic  15.8 us (7%)
    ppermute x16, waiting for transfers between devices, shifted_copies(): copies.append(lax.ppermute(block, axis_name, pairs))  42.9 us
    ppermute x16, starting transfers between devices, shifted_copies(): copies.append(lax.ppermute(block, axis_name, pairs))  21.4 us
    reduce_scatter x1, waiting for transfers between devices, shards(): lax.psum_scatter(partial_out.astype(jnp.bfloat16), 'hid', scatter_dimensi...  18.4 us
    unnamed x105, local copies, waits for them, and re-layouts  17.3 us
    dynamic_slice x9, local copies, waits for them, and re-layouts, shards(): lax.dynamic_index_in_dim(gathered, prefix_group[0, seg], 0, keepdims=False)  15.3 us
    dot_general x8, matrix products, shards(): jnp.einsum('tkgd,skd->kgts', query_window, chosen[..., :head_dim], prefer...  11.3 us
    dot_general x8, matrix products, shards(): jnp.einsum('kgts,skd->kgtd', fresh.astype(jnp.bfloat16), chosen[..., head...  11 us
    dynamic_update_slice x8, local copies, waits for them, and re-layouts, shards(): lax.dynamic_update_slice_in_dim(totals, jnp.where(inside[None, None], new...  6.19 us
  transfers between devices with their start and end apart: 19, of which 3 were waited for; matrix products, arithmetic and copies ran while one was open for 39% of the time, Pallas kernels for 0%

profile of v2, /device:TPU:0, one launch (start us, length us, event | category | flops | bytes accessed | tf_op | source)
XLA Modules:
  0.0 223.1 jit_solution(13820979250731167173)
XLA Ops:
  7.2 2.5 %copy.84 = bf16[2,1024,2,128]{3,1,2,0:T(8,128)(2,1)} copy(bf16[2,1024,2,128]{3,2,1,0:T(2,128)(2,1)} %param.17) | data formatting | bytes 2097152 | tf_op args[3]
  9.8 3.1 %collective-permute-start = (bf16[256,256]{1,0:T(8,128)(2,1)S(1)}, bf16[256,256]{1,0:T(8,128)(2,1)S(1)}, u32[]{:S(2)}, u32[]{:S(2)}) collective-permute-start(bf16[256,256]{1,0:T(8,128)(2,1)S(1)} %copy-done.13), channel_id=1, source_target_pairs={{0,1},{1,2},{2,3},{3,0},{4,5},{5,6},{6,7},{7,4},{8,9},{9,10},{10,1... | collective-permute-start | bytes 393224 | tf_op jit(solution)/shard_map/ppermute | solution.py:69
  12.9 2.1 collective-permute-start.2
  16.1 1.4 collective-permute-start.12
  44.9 1.9 constant_dynamic-update-slice_fusion.7
  46.8 1.5 collective-permute-start.11
  48.3 2.4 %collective-permute-start.10 = (bf16[2,128,1024]{2,1,0:T(8,128)(2,1)}, bf16[2,128,1024]{2,1,0:T(8,128)(2,1)}, u32[]{:S(2)}, u32[]{:S(2)}) collective-permute-start(bf16[2,128,1024]{2,1,0:T(8,128)(2,1)} %param.27), channel_id=1, source_target_pairs={{0,8},{4,12},{8,16},{12,20},{16,24},{20,28},{24,0},{28,4},{1,9},{5... | collective-permute-start | bytes 1572872 | tf_op jit(solution)/shard_map/ppermute | solution.py:69
  55.2 36.3 %collective-permute-done.9 = bf16[2,128,1024]{2,1,0:T(8,128)(2,1)} collective-permute-done((bf16[2,128,1024]{2,1,0:T(8,128)(2,1)}, bf16[2,128,1024]{2,1,0:T(8,128)(2,1)}, u32[]{:S(2)}, u32[]{:S(2)}) %collective-permute-start.9) | collective-permute-done | bytes 524320 | tf_op jit(solution)/shard_map/ppermute | solution.py:69
  91.5 1.9 collective-permute-start.7
  93.3 1.9 constant_dynamic-update-slice_fusion.6
  95.2 1.9 constant_dynamic-update-slice_fusion.5
  97.1 3.8 %collective-permute-start.8 = (bf16[256,1024]{1,0:T(8,128)(2,1)}, bf16[256,1024]{1,0:T(8,128)(2,1)}, u32[]{:S(2)}, u32[]{:S(2)}) collective-permute-start(bf16[256,1024]{1,0:T(8,128)(2,1)} %param.22), channel_id=1, source_target_pairs={{0,3},{1,0},{2,1},{3,2},{4,7},{5,4},{6,5},{7,6},{8,11},{9,8},{10,9... | collective-permute-start | bytes 1572872 | tf_op jit(solution)/shard_map/ppermute | solution.py:69
  101.7 1.2 collective-permute-start.14
  104.6 3.7 %constant_dynamic-slice_fusion.8 = (bf16[1,1024,2,128]{3,1,2,0:T(8,128)(2,1)}, bf16[1,1024,2,128]{3,1,2,0:T(8,128)(2,1)}, bf16[1,1024,2,128]{3,1,2,0:T(8,128)(2,...) fusion(bf16[16,1024,2,128]{3,1,2,0:T(8,128)(2,1)} %all-gather.3, ...), kind=kLoop, calls=%fused_computation.216 | loop fusion | bytes 8388640 | tf_op jit(solution)/shard_map/jit(dynamic_index_in_dim)/dynamic_slice | solution.py:146
  108.3 1.2 copy.99
  109.5 2.1 copy.97
  111.6 2.1 copy.95
  113.7 2.1 copy.93
  119.9 1.5 bitcast_reduce_fusion.7
  122.9 1.4 fusion.49
  125.7 1.5 bitcast_reduce_fusion.6
  128.7 1.4 fusion.48
  130.1 1.1 dynamic_update_slice.73
  131.3 1.1 dynamic_update_slice.87
  132.4 1.5 bitcast_reduce_fusion.5
  135.4 1.5 fusion.47
  136.9 1.1 dynamic_update_slice.75
  139.1 1.5 bitcast_reduce_fusion.4
  142.1 1.4 fusion.46
  143.6 1.1 dynamic_update_slice.77
  145.8 1.5 bitcast_reduce_fusion.3
  148.8 1.4 fusion.45
  150.3 1.1 dynamic_update_slice.79
  152.5 1.5 bitcast_reduce_fusion.2
  155.4 1.7 bitcast_reduce_fusion.1
  157.7 1.2 fusion.44
  163.9 2.1 fusion.42
  167.1 1.2 collective-permute-start.4
  168.3 1.2 collective-permute-start.3
  169.6 1.9 constant_dynamic-update-slice_fusion.1
  171.5 1.9 constant_dynamic-update-slice_fusion
  173.4 6.6 %collective-permute-done.4 = bf16[256,256]{0,1:T(8,128)(2,1)S(1)} collective-permute-done((bf16[256,256]{0,1:T(8,128)(2,1)S(1)}, bf16[256,256]{0,1:T(8,128)(2,1)S(1)}, u32[]{:S(2)}, u32[]{:S(2)}) %collective-permute-start.4) | collective-permute-done | bytes 131104 | tf_op jit(solution)/shard_map/ppermute | solution.py:69
  180.0 2.4 %fusion.50 = (f32[256]{0:T(256)S(1)}, bf16[256,1024]{1,0:T(8,128)(2,1)S(1)}) fusion(bf16[256,1024]{1,0:T(8,128)(2,1)} %collective-permute-done.8, bf16[256,1024]{1,0:T(8,128)(2,1)} %collective-permute-done.7, bf16[256,1024]{1,0:T(8,128)(2,1)} %collective-permute-done.6, bf16[256,1024]{1,0:T(8,128)(2,1)} %param.22, ...), kind=kOutput, calls=%fused_computation.83 | convolution fusion | flops 550764288 | bytes 3671040 | tf_op jit(solution)/shard_map/dot_general | solution.py:193
  182.4 3.6 %fusion.1 = f32[256,16,128]{2,0,1:T(8,128)S(1)} fusion(bf16[16,2,1024,128]{3,2,0,1:T(8,128)(2,1)} %all-gather.5.cloned.1.call-done, bf16[256,1024]{1,0:T(8,128)(2,1)S(1)} %get-tuple-element.101, f32[1024]{0:T(1024)S(1)} %copy-done.44, f32[256]{0:T(256)S(1)} %add_rsqrt_fusion), kind=kOutput, calls=%fused_computation.6 | convolution fusion | flops 1074790400 | bytes 6820864 | tf_op jit(solution)/shard_map/td,edf->tef/dot_general | solution.py:211
  187.1 1.7 multiply_convert_fusion
  189.7 4.3 %fusion.38 = bf16[256,1024]{1,0:T(8,128)(2,1)} fusion(bf16[16,128,1024]{2,1,0:T(8,128)(2,1)} %constant_dynamic-update-slice_fusion, bf16[16,256,128]{2,1,0:T(8,128)(2,1)S(1)} %gather_fusion.1, pred[16]{0:T(512)(128)(4,1)S(1)} %copy-done.46), kind=kOutput, calls=%fused_computation.65 | convolution fusion | flops 1074528256 | bytes 5767184 | tf_op jit(solution)/shard_map/tef,efd->td/dot_general | solution.py:218
  196.6 18.4 %reduce-scatter.2.cloned.1.call-done = bf16[256,256]{1,0:T(8,128)(2,1)} async-done(((bf16[256,1024]{1,0:T(8,128)(2,1)}), bf16[256,256]{1,0:T(8,128)(2,1)}) %reduce-scatter.2.cloned.1.call-update) | async-done | bytes 131088 | tf_op jit(solution)/shard_map/reduce_scatter | solution.py:221
  215.0 1.6 add_convert_fusion
  (217 shorter events, 43.3 us)
Async XLA Ops:
  7.2 45.5 %copy-start = (bf16[1024,256]{1,0:T(8,128)(2,1)S(1)}, bf16[1024,256]{1,0:T(8,128)(2,1)}, u32[]{:S(2)}) copy-start(bf16[1024,256]{1,0:T(8,128)(2,1)} %param.21) | copy-start | bytes 1572868
  7.2 2.6 %copy-start.13 = (bf16[256,256]{1,0:T(8,128)(2,1)S(1)}, bf16[256,256]{1,0:T(8,128)(2,1)}, u32[]{:S(2)}) copy-start(bf16[256,256]{1,0:T(8,128)(2,1)} %param.14) | copy-start | bytes 393220
  7.2 10.3 %copy-start.7 = (bf16[2,2,1024,128]{3,2,1,0:T(8,128)(2,1)S(1)}, bf16[2,2,1024,128]{3,2,1,0:T(8,128)(2,1)}, u32[]{:S(2)}) copy-start(bf16[2,2,1024,128]{3,2,1,0:T(8,128)(2,1)} %param.26) | copy-start | bytes 3145732
  7.2 97.4 %all-gather.3.cloned.1.call-start = ((), (), s32[]{:S(2)}) async-start(), calls=%async_computation.1 | async-start | bytes 9437184 | tf_op jit(solution)/shard_map/all_gather | solution.py:141
  9.7 9.1 %copy-start.18 = (s32[1,256]{1,0:T(1,128)S(1)}, s32[1,256]{1,0:T(1,128)}, u32[]{:S(2)}) copy-start(s32[1,256]{1,0:T(1,128)} %param.15) | copy-start | bytes 3076
  9.7 16.2 %copy-start.20 = (s32[1,8]{1,0:T(1,128)S(1)}, s32[1,8]{1,0:T(1,128)}, u32[]{:S(2)}) copy-start(s32[1,8]{1,0:T(1,128)} %param.16) | copy-start | bytes 100
  9.7 18.4 %copy-start.38 = (f32[256,8]{0,1:T(8,128)S(1)}, f32[256,8]{0,1:T(8,128)}, u32[]{:S(2)}) copy-start(f32[256,8]{0,1:T(8,128)} %param.25) | copy-start | bytes 24580
  9.7 18.4 %copy-start.39 = (s32[256,8]{0,1:T(8,128)S(1)}, s32[256,8]{0,1:T(8,128)}, u32[]{:S(2)}) copy-start(s32[256,8]{0,1:T(8,128)} %param.24) | copy-start | bytes 24580
  9.8 172.6 %all-gather.5.cloned.1.call-start = ((), (), s32[]{:S(2)}) async-start(), calls=%async_computation.2 | async-start | bytes 9437184 | tf_op jit(solution)/shard_map/all_gather | solution.py:199
  9.8 37.0 %collective-permute-start = (bf16[256,256]{1,0:T(8,128)(2,1)S(1)}, bf16[256,256]{1,0:T(8,128)(2,1)S(1)}, u32[]{:S(2)}, u32[]{:S(2)}) collective-permute-start(bf16[256,256]{1,0:T(8,128)(2,1)S(1)} %copy-done.13), channel_id=1, source_target_pairs={{0,1},{1,2},{2,3},{3,0},{4,5},{5,6},{6,7},{7,4},{8,9},{9,10},{10,1... | collective-permute-start | bytes 393224 | tf_op jit(solution)/shard_map/ppermute | solution.py:69
  12.9 35.4 %collective-permute-start.2 = (bf16[256,256]{1,0:T(8,128)(2,1)S(1)}, bf16[256,256]{1,0:T(8,128)(2,1)S(1)}, u32[]{:S(2)}, u32[]{:S(2)}) collective-permute-start(bf16[256,256]{1,0:T(8,128)(2,1)S(1)} %copy-done.13), channel_id=1, source_target_pairs={{0,3},{1,0},{2,1},{3,2},{4,7},{5,4},{6,5},{7,6},{8,11},{9,8},{10,9... | collective-permute-start | bytes 393224 | tf_op jit(solution)/shard_map/ppermute | solution.py:69
  15.0 35.7 %collective-permute-start.1 = (bf16[256,256]{1,0:T(8,128)(2,1)S(1)}, bf16[256,256]{1,0:T(8,128)(2,1)}, u32[]{:S(2)}, u32[]{:S(2)}) collective-permute-start(bf16[256,256]{1,0:T(8,128)(2,1)S(1)} %copy-done.13), channel_id=1, source_target_pairs={{0,2},{1,3},{2,0},{3,1},{4,6},{5,7},{6,4},{7,5},{8,10},{9,11},{10,... | collective-permute-start | bytes 393224 | tf_op jit(solution)/shard_map/ppermute | solution.py:69
  16.0 87.8 %collective-permute-start.13 = (bf16[2,128,1024]{2,1,0:T(8,128)(2,1)}, bf16[2,128,1024]{2,1,0:T(8,128)(2,1)S(1)}, u32[]{:S(2)}, u32[]{:S(2)}) collective-permute-start(bf16[2,128,1024]{2,1,0:T(8,128)(2,1)} %param.27), channel_id=1, source_target_pairs={{0,20},{4,24},{8,28},{12,0},{16,4},{20,8},{24,12},{28,16},{1,21},{... | collective-permute-start | bytes 1572872 | tf_op jit(solution)/shard_map/ppermute | solution.py:69
  16.1 85.6 %collective-permute-start.12 = (bf16[2,128,1024]{2,1,0:T(8,128)(2,1)}, bf16[2,128,1024]{2,1,0:T(8,128)(2,1)S(1)}, u32[]{:S(2)}, u32[]{:S(2)}) collective-permute-start(bf16[2,128,1024]{2,1,0:T(8,128)(2,1)} %param.27), channel_id=1, source_target_pairs={{0,16},{4,20},{8,24},{12,28},{16,0},{20,4},{24,8},{28,12},{1,17},{... | collective-permute-start | bytes 1572872 | tf_op jit(solution)/shard_map/ppermute | solution.py:69
  18.5 196.5 %reduce-scatter.2.cloned.1.call-start = ((), (), s32[]{:S(2)}) async-start(), calls=%async_computation.3 | async-start | bytes 655360 | tf_op jit(solution)/shard_map/reduce_scatter | solution.py:221
  28.1 93.3 %copy-start.36 = (pred[128]{0:T(512)(128)(4,1)}, pred[128]{0:T(512)(128)(4,1)S(1)}, u32[]{:S(2)}) copy-start(pred[128]{0:T(512)(128)(4,1)S(1)} %get-tuple-element.72) | copy-start | bytes 388
  46.8 50.3 %collective-permute-start.11 = (bf16[2,128,1024]{2,1,0:T(8,128)(2,1)}, bf16[2,128,1024]{2,1,0:T(8,128)(2,1)S(1)}, u32[]{:S(2)}, u32[]{:S(2)}) collective-permute-start(bf16[2,128,1024]{2,1,0:T(8,128)(2,1)} %param.27), channel_id=1, source_target_pairs={{0,12},{4,16},{8,20},{12,24},{16,28},{20,0},{24,4},{28,8},{1,13},{... | collective-permute-start | bytes 1572872 | tf_op jit(solution)/shard_map/ppermute | solution.py:69
  48.3 46.9 %collective-permute-start.10 = (bf16[2,128,1024]{2,1,0:T(8,128)(2,1)}, bf16[2,128,1024]{2,1,0:T(8,128)(2,1)}, u32[]{:S(2)}, u32[]{:S(2)}) collective-permute-start(bf16[2,128,1024]{2,1,0:T(8,128)(2,1)} %param.27), channel_id=1, source_target_pairs={{0,8},{4,12},{8,16},{12,20},{16,24},{20,28},{24,0},{28,4},{1,9},{5... | collective-permute-start | bytes 1572872 | tf_op jit(solution)/shard_map/ppermute | solution.py:69
  50.7 40.8 %collective-permute-start.9 = (bf16[2,128,1024]{2,1,0:T(8,128)(2,1)}, bf16[2,128,1024]{2,1,0:T(8,128)(2,1)}, u32[]{:S(2)}, u32[]{:S(2)}) collective-permute-start(bf16[2,128,1024]{2,1,0:T(8,128)(2,1)} %param.27), channel_id=1, source_target_pairs={{0,4},{4,8},{8,12},{12,16},{16,20},{20,24},{24,28},{28,0},{1,5},{5... | collective-permute-start | bytes 1572872 | tf_op jit(solution)/shard_map/ppermute | solution.py:69
  91.5 75.2 %collective-permute-start.7 = (bf16[256,1024]{1,0:T(8,128)(2,1)}, bf16[256,1024]{1,0:T(8,128)(2,1)}, u32[]{:S(2)}, u32[]{:S(2)}) collective-permute-start(bf16[256,1024]{1,0:T(8,128)(2,1)} %param.22), channel_id=1, source_target_pairs={{0,2},{1,3},{2,0},{3,1},{4,6},{5,7},{6,4},{7,5},{8,10},{9,11},{10,... | collective-permute-start | bytes 1572872 | tf_op jit(solution)/shard_map/ppermute | solution.py:69
  95.2 78.1 %collective-permute-start.6 = (bf16[256,1024]{1,0:T(8,128)(2,1)}, bf16[256,1024]{1,0:T(8,128)(2,1)}, u32[]{:S(2)}, u32[]{:S(2)}) collective-permute-start(bf16[256,1024]{1,0:T(8,128)(2,1)} %param.22), channel_id=1, source_target_pairs={{0,1},{1,2},{2,3},{3,0},{4,5},{5,6},{6,7},{7,4},{8,9},{9,10},{10,1... | collective-permute-start | bytes 1572872 | tf_op jit(solution)/shard_map/ppermute | solution.py:69
  97.1 76.2 %collective-permute-start.8 = (bf16[256,1024]{1,0:T(8,128)(2,1)}, bf16[256,1024]{1,0:T(8,128)(2,1)}, u32[]{:S(2)}, u32[]{:S(2)}) collective-permute-start(bf16[256,1024]{1,0:T(8,128)(2,1)} %param.22), channel_id=1, source_target_pairs={{0,3},{1,0},{2,1},{3,2},{4,7},{5,4},{6,5},{7,6},{8,11},{9,8},{10,9... | collective-permute-start | bytes 1572872 | tf_op jit(solution)/shard_map/ppermute | solution.py:69
  101.7 65.4 %collective-permute-start.14 = (bf16[2,128,1024]{2,1,0:T(8,128)(2,1)}, bf16[2,128,1024]{2,1,0:T(8,128)(2,1)}, u32[]{:S(2)}, u32[]{:S(2)}) collective-permute-start(bf16[2,128,1024]{2,1,0:T(8,128)(2,1)} %param.27), channel_id=1, source_target_pairs={{0,24},{4,28},{8,0},{12,4},{16,8},{20,12},{24,16},{28,20},{1,25},{... | collective-permute-start | bytes 1572872 | tf_op jit(solution)/shard_map/ppermute | solution.py:69
  103.7 64.6 %collective-permute-start.15 = (bf16[2,128,1024]{2,1,0:T(8,128)(2,1)}, bf16[2,128,1024]{2,1,0:T(8,128)(2,1)}, u32[]{:S(2)}, u32[]{:S(2)}) collective-permute-start(bf16[2,128,1024]{2,1,0:T(8,128)(2,1)} %param.27), channel_id=1, source_target_pairs={{0,28},{4,0},{8,4},{12,8},{16,12},{20,16},{24,20},{28,24},{1,29},{... | collective-permute-start | bytes 1572872 | tf_op jit(solution)/shard_map/ppermute | solution.py:69
  124.3 2.9 %copy-start.34 = (pred[128]{0:T(512)(128)(4,1)S(1)}, pred[128]{0:T(512)(128)(4,1)}, u32[]{:S(2)}) copy-start(pred[128]{0:T(512)(128)(4,1)} %get-tuple-element.71) | copy-start | bytes 388
  130.1 3.7 %copy-start.32 = (pred[128]{0:T(512)(128)(4,1)S(1)}, pred[128]{0:T(512)(128)(4,1)}, u32[]{:S(2)}) copy-start(pred[128]{0:T(512)(128)(4,1)} %get-tuple-element.70) | copy-start | bytes 388
  132.4 2.0 copy-start.33
  136.9 3.7 %copy-start.30 = (pred[128]{0:T(512)(128)(4,1)S(1)}, pred[128]{0:T(512)(128)(4,1)}, u32[]{:S(2)}) copy-start(pred[128]{0:T(512)(128)(4,1)} %get-tuple-element.69) | copy-start | bytes 388
  143.6 3.7 %copy-start.28 = (pred[128]{0:T(512)(128)(4,1)S(1)}, pred[128]{0:T(512)(128)(4,1)}, u32[]{:S(2)}) copy-start(pred[128]{0:T(512)(128)(4,1)} %get-tuple-element.68) | copy-start | bytes 388
  145.8 2.0 copy-start.29
  150.3 3.8 %copy-start.23 = (pred[128]{0:T(512)(128)(4,1)S(1)}, pred[128]{0:T(512)(128)(4,1)}, u32[]{:S(2)}) copy-start(pred[128]{0:T(512)(128)(4,1)} %get-tuple-element.67) | copy-start | bytes 388
  154.1 2.9 %copy-start.21 = (f32[2,2,128]{2,1,0:T(2,128)}, f32[2,2,128]{2,1,0:T(2,128)S(1)}, u32[]{:S(2)}) copy-start(f32[2,2,128]{2,1,0:T(2,128)S(1)} %get-tuple-element.37) | copy-start | bytes 6148
  154.4 2.6 %copy-start.24 = (pred[128]{0:T(512)(128)(4,1)S(1)}, pred[128]{0:T(512)(128)(4,1)}, u32[]{:S(2)}) copy-start(pred[128]{0:T(512)(128)(4,1)} %get-tuple-element.67) | copy-start | bytes 388
  154.5 2.6 %copy-start.25 = (pred[128]{0:T(512)(128)(4,1)S(1)}, pred[128]{0:T(512)(128)(4,1)}, u32[]{:S(2)}) copy-start(pred[128]{0:T(512)(128)(4,1)} %get-tuple-element.73) | copy-start | bytes 388
  154.5 3.3 %copy-start.6 = (bf16[1,1024,2,128]{1,3,2,0:T(8,128)(2,1)S(1)}, bf16[1,1024,2,128]{1,3,2,0:T(8,128)(2,1)}, u32[]{:S(2)}) copy-start(bf16[1,1024,2,128]{1,3,2,0:T(8,128)(2,1)} %copy.95) | copy-start | bytes 1572868
  155.4 2.4 %copy-start.4 = (f32[2,1024,128,2]{2,1,3,0:T(8,128)S(1)}, f32[2,1024,128,2]{2,1,3,0:T(8,128)}, u32[]{:S(2)}) copy-start(f32[2,1024,128,2]{2,1,3,0:T(8,128)} %copy-done.3) | copy-start | bytes 6291460
  157.7 2.7 %copy-start.26 = (pred[128]{0:T(512)(128)(4,1)S(1)}, pred[128]{0:T(512)(128)(4,1)}, u32[]{:S(2)}) copy-start(pred[128]{0:T(512)(128)(4,1)} %get-tuple-element.73) | copy-start | bytes 388
  163.9 16.1 %copy-start.9 = (bf16[256,256]{1,0:T(8,128)(2,1)S(1)}, bf16[256,256]{1,0:T(8,128)(2,1)}, u32[]{:S(2)}) copy-start(bf16[256,256]{1,0:T(8,128)(2,1)} %copy-done.8) | copy-start | bytes 393220
  166.6 6.7 %collective-permute-start.5 = (bf16[256,256]{0,1:T(8,128)(2,1)S(1)}, bf16[256,256]{0,1:T(8,128)(2,1)S(1)}, u32[]{:S(2)}, u32[]{:S(2)}) collective-permute-start(bf16[256,256]{0,1:T(8,128)(2,1)S(1)} %bitcast.315), channel_id=1, source_target_pairs={{0,3},{1,0},{2,1},{3,2},{4,7},{5,4},{6,5},{7,6},{8,11},{9,8},{10,9... | collective-permute-start | bytes 393224 | tf_op jit(solution)/shard_map/ppermute | solution.py:69
  167.1 12.9 %collective-permute-start.4 = (bf16[256,256]{0,1:T(8,128)(2,1)S(1)}, bf16[256,256]{0,1:T(8,128)(2,1)S(1)}, u32[]{:S(2)}, u32[]{:S(2)}) collective-permute-start(bf16[256,256]{0,1:T(8,128)(2,1)S(1)} %bitcast.316), channel_id=1, source_target_pairs={{0,2},{1,3},{2,0},{3,1},{4,6},{5,7},{6,4},{7,5},{8,10},{9,11},{10,... | collective-permute-start | bytes 393224 | tf_op jit(solution)/shard_map/ppermute | solution.py:69
  168.3 11.6 %collective-permute-start.3 = (bf16[256,256]{0,1:T(8,128)(2,1)S(1)}, bf16[256,256]{0,1:T(8,128)(2,1)S(1)}, u32[]{:S(2)}, u32[]{:S(2)}) collective-permute-start(bf16[256,256]{0,1:T(8,128)(2,1)S(1)} %bitcast.317), channel_id=1, source_target_pairs={{0,1},{1,2},{2,3},{3,0},{4,5},{5,6},{6,7},{7,4},{8,9},{9,10},{10,1... | collective-permute-start | bytes 393224 | tf_op jit(solution)/shard_map/ppermute | solution.py:69
  173.3 9.1 %copy-start.44 = (f32[1024]{0:T(1024)S(1)}, f32[1024]{0:T(1024)}, u32[]{:S(2)}) copy-start(f32[1024]{0:T(1024)} %param.23) | copy-start | bytes 12292
  182.4 3.7 %copy-start.22 = (f32[256,16]{0,1:T(8,128)S(1)}, f32[256,16]{0,1:T(8,128)}, u32[]{:S(2)}) copy-start(f32[256,16]{0,1:T(8,128)} %select_reduce_fusion) | copy-start | bytes 49156
  182.4 4.7 %copy-start.41 = (bf16[16,2,1024,128]{3,2,0,1:T(8,128)(2,1)S(1)}, bf16[16,2,1024,128]{3,2,0,1:T(8,128)(2,1)}, u32[]{:S(2)}) copy-start(bf16[16,2,1024,128]{3,2,0,1:T(8,128)(2,1)} %all-gather.5.cloned.1.call-done) | copy-start | bytes 25165828
  189.6 4.4 %copy-start.45 = (s32[1,2]{1,0:T(1,128)S(1)}, s32[1,2]{1,0:T(1,128)}, u32[]{:S(2)}) copy-start(s32[1,2]{1,0:T(1,128)} %param.18) | copy-start | bytes 28
  189.6 5.3 %copy-start.15 = (bf16[256,2,32]{0,2,1:T(8,128)(2,1)S(1)}, bf16[256,2,32]{0,2,1:T(8,128)(2,1)}, u32[]{:S(2)}) copy-start(bf16[256,2,32]{0,2,1:T(8,128)(2,1)} %copy-done.14) | copy-start | bytes 98308
  189.7 5.3 %copy-start.17 = (bf16[256,2,32]{0,2,1:T(8,128)(2,1)S(1)}, bf16[256,2,32]{0,2,1:T(8,128)(2,1)}, u32[]{:S(2)}) copy-start(bf16[256,2,32]{0,2,1:T(8,128)(2,1)} %copy-done.16) | copy-start | bytes 98308
  189.7 26.9 %copy-start.1 = (bf16[1024,256]{1,0:T(8,128)(2,1)S(1)}, bf16[1024,256]{1,0:T(8,128)(2,1)}, u32[]{:S(2)}) copy-start(bf16[1024,256]{1,0:T(8,128)(2,1)} %param.21) | copy-start | bytes 1572868
  (18 other events, 21.5 us)
Sparse Core Ops, SparseCore 0:
  9.9 93.2 all-gather.2
  105.1 56.3 all-gather.4
  194.2 20.8 reduce-scatter.1
